TPU v7x, 512 devices: a whole 4x4x16 slice. The times are simulated.
512 devices in a mesh: head: 8 (over x, core), expert: 64 (over z, y).
Axes of the slice: x: 4, y: 4, z: 16, core: 2. Of those that a mesh axis runs over, the one named last changes fastest.
Arguments:
- q_latent: bfloat16 [512, 64, 512], P('expert', 'head'), may hold values from -16 to 16
- q_rotary: bfloat16 [512, 64, 64], P('expert', 'head'), may hold values from -3 to 3
- cache_latent: bfloat16 [512, 128, 512], P('expert'), may hold values from -5 to 5
- cache_rotary: bfloat16 [512, 64, 128], P('expert'), may hold values from -5 to 5
- lengths: int32 [512], P('expert'), may hold values from 16 to 128, as said below
- w_value_out: bfloat16 [32768, 5120], P('head', 'expert'), may hold values from -0.25 to 0.25
- resid: bfloat16 [512, 5120], P('expert'), may hold values from -8 to 8
- norm_gain: float32 [5120], replicated, may hold values from 0.1 to 1.9
- route_ids: int32 [512, 6], P('expert'), may hold values from 0 to 63, as said below
- route_weights: float32 [512, 6], P('expert'), may hold values from 0.1 to 0.6
- w_gate_up: bfloat16 [64, 2, 768, 5120], P('expert', None, 'head'), may hold values from -0.078125 to 0.078125
- w_down: bfloat16 [64, 768, 5120], P('expert', 'head'), may hold values from -0.21875 to 0.21875
Outputs:
- mixed_out: float32 [512, 5120], P('expert', 'head')
Inputs may be any that keep to these rules, and one draw needn't show every extreme that they name: `lengths`: slots at positions below a sequence's length are valid; some sequence has length 128. `route_ids`: each row names 6 different experts. Among the rows of one device (aligned blocks of 8 rows) no expert is named by more than 2 rows, and one expert is named by exactly 2 rows in every block.
All inputs are finite; a program needn't handle non-finite values.
Results may differ from a plain program's by a relative error of at most 0.0046.
Values may be sent and summed in bfloat16 or wider, within the bound.
No kernel may reach another device: no remote copies, remote signals or barrier semaphores. Data moves between devices by JAX's collectives and lax.ppermute only.
A program may use at most 64 MiB of HBM per device.

v0:
```python
import jax
import jax.numpy as jnp
from jax import lax
from jax.sharding import PartitionSpec as P

softmax_scale = 192.0 ** (-0.5)
norm_epsilon = 1e-06


def attend(q_latent, q_rotary, cache_latent, cache_rotary, lengths):
    scores = jnp.einsum("shl,scl->shc", q_latent, cache_latent, preferred_element_type=jnp.float32)
    scores = scores + jnp.einsum(
        "shr,src->shc", q_rotary, cache_rotary, preferred_element_type=jnp.float32
    )
    scores = scores * softmax_scale
    position = lax.broadcasted_iota(jnp.int32, scores.shape, 2)
    scores = jnp.where(position < lengths[:, None, None], scores, -1e30)
    highest = jnp.max(scores, axis=2, keepdims=True)
    weights = jnp.exp(scores - highest)
    probs = (weights / jnp.sum(weights, axis=2, keepdims=True)).astype(jnp.bfloat16)
    return jnp.einsum(
        "shc,scl->shl", probs, cache_latent, preferred_element_type=jnp.float32
    ).astype(jnp.bfloat16)


def on_device(
    q_latent,
    q_rotary,
    cache_latent,
    cache_rotary,
    lengths,
    w_value_out,
    resid,
    norm_gain,
    route_ids,
    route_weights,
    w_gate_up,
    w_down,
):
    seq_local = q_latent.shape[0]
    latent_out = attend(q_latent, q_rotary, cache_latent, cache_rotary, lengths)
    flattened = latent_out.reshape(seq_local, -1)
    column_terms = jnp.dot(
        lax.all_gather(flattened, "expert", axis=0, tiled=True),
        w_value_out,
        preferred_element_type=jnp.float32,
    )
    column_sums = lax.psum(column_terms, "head")
    attention = lax.all_to_all(
        column_sums.astype(jnp.bfloat16), "expert", split_axis=0, concat_axis=1, tiled=True
    )
    stream = resid.astype(jnp.float32) + attention.astype(jnp.float32)
    mean_square = jnp.mean(stream * stream, axis=1, keepdims=True)
    normed = (stream * lax.rsqrt(mean_square + norm_epsilon) * norm_gain).astype(jnp.bfloat16)
    expert_count = lax.axis_size("expert")
    top_count = route_ids.shape[1]
    capacity = max(2, -(-(seq_local * top_count) // expert_count))
    flat_ids = route_ids.reshape(-1)
    one_hot = (flat_ids[:, None] == jnp.arange(expert_count, dtype=jnp.int32)[None, :]).astype(
        jnp.int32
    )
    earlier = jnp.cumsum(one_hot, axis=0) - one_hot
    slot_index = jnp.sum(earlier * one_hot, axis=1)
    target = (flat_ids * capacity + slot_index).reshape(seq_local, top_count)
    places = jnp.arange(expert_count * capacity, dtype=jnp.int32)
    matches = target[None, :, :] == places[:, None, None]
    selector = jnp.sum(matches.astype(jnp.int32), axis=2).astype(jnp.bfloat16)
    blending = jnp.sum(jnp.where(matches, route_weights[None, :, :], 0.0), axis=2)
    gate_up = w_gate_up[0]
    down_local = w_down[0]
    col_width = stream.shape[1] // lax.axis_size("head")
    offset = lax.axis_index("head") * col_width
    normed_cols = lax.dynamic_slice_in_dim(normed, offset, col_width, 1)
    outgoing = jnp.dot(selector, normed_cols, preferred_element_type=jnp.float32).astype(
        jnp.bfloat16
    )
    outgoing = outgoing.reshape(expert_count, capacity, -1)
    arrived = lax.all_to_all(outgoing, "expert", split_axis=0, concat_axis=0, tiled=True)
    arrived_cols = arrived.reshape(-1, arrived.shape[2])
    flat_rows = lax.all_gather(arrived_cols, "head", axis=1, tiled=True)
    projected = jnp.einsum("rd,gfd->rgf", flat_rows, gate_up, preferred_element_type=jnp.float32)
    hidden = (jax.nn.silu(projected[:, 0]) * projected[:, 1]).astype(jnp.bfloat16)
    partial_rows = jnp.dot(hidden, down_local, preferred_element_type=jnp.float32)
    summed_cols = lax.psum_scatter(
        partial_rows.astype(jnp.bfloat16), "head", scatter_dimension=1, tiled=True
    )
    summed_rows = summed_cols.reshape(expert_count, capacity, -1)
    returned = lax.all_to_all(summed_rows, "expert", split_axis=0, concat_axis=0, tiled=True)
    back_rows = returned.reshape(expert_count * capacity, -1).astype(jnp.float32)
    mixture = jnp.dot(blending.T, back_rows, precision=lax.Precision.HIGHEST)
    stream_cols = lax.dynamic_slice_in_dim(stream, offset, col_width, 1)
    return stream_cols + mixture


def solution(mesh):
    placed = (
        P("expert", "head", None),
        P("expert", "head", None),
        P("expert", None, None),
        P("expert", None, None),
        P("expert"),
        P("head", "expert"),
        P("expert", None),
        P(),
        P("expert", None),
        P("expert", None),
        P("expert", None, "head", None),
        P("expert", "head", None),
    )
    return jax.shard_map(
        on_device, mesh=mesh, in_specs=placed, out_specs=P("expert", "head"), check_vma=False
    )
```

profile of v0, /device:TPU:7, one launch (start us, length us, event | category | flops | bytes accessed | tf_op | source)
XLA Modules:
  0.0 349.5 jit_solution(5322238232163485525)
XLA Ops:
  6.5 1.8 fusion.21
  8.3 1.1 fusion.8
  9.4 0.2 fusion.20
  9.6 1.5 fusion.4
  11.1 0.7 copy.24
  11.8 0.1 eq.28
  12.0 0.2 select_reduce_fusion.1
  12.3 142.5 %all-gather.3.cloned.1.call-done = bf16[512,4096]{1,0:T(8,128)(2,1)} async-done(((bf16[8,4096]{1,0:T(8,128)(2,1)}), bf16[512,4096]{1,0:T(8,128)(2,1)}) %all-gather.3.cloned.1.call-update) | async-done | bytes 4194320 | tf_op jit(solution)/shard_map/all_gather | solution.py:44
  154.8 3.6 %fusion.22 = f32[512,80]{0,1:T(8,128)S(1)} fusion(bf16[512,4096]{1,0:T(8,128)(2,1)} %all-gather.3.cloned.1.call-done, bf16[4096,80]{0,1:T(8,128)(2,1)S(1)} %copy-done.1), kind=kOutput, calls=%fused_computation.40 | convolution fusion | flops 335544320 | bytes 5013504 | tf_op jit(solution)/shard_map/dot_general | solution.py:43
  158.4 31.2 %all-reduce.1 = bf16[512,80]{0,1:T(8,128)(2,1)S(1)} all-reduce(f32[512,80]{0,1:T(8,128)S(1)} %fusion.22), channel_id=1, replica_groups=mesh['head'=8,'expert'=64] {'head'}, use_global_device_ids=true, to_apply=%region_2.3 | all-reduce | flops 40960 | bytes 245760 | tf_op jit(solution)/shard_map/psum | solution.py:48
  189.6 0.7 copy.18
  190.4 8.6 %all-to-all-start = ((bf16[64,8,80]{2,1,0:T(8,128)(2,1)}), bf16[64,8,80]{2,1,0:T(8,128)(2,1)S(1)}, u32[]{:S(2)}, u32[]{:S(2)}) async-start(bf16[64,8,80]{2,1,0:T(8,128)(2,1)} %bitcast), calls=%async_computation | async-start | bytes 262144 | tf_op jit(solution)/shard_map/all_to_all | solution.py:49
  199.0 0.1 copy.20
  199.1 0.8 dynamic-slice
  200.0 15.2 %all-to-all-done = bf16[64,8,80]{2,1,0:T(8,128)(2,1)S(1)} async-done(((bf16[64,8,80]{2,1,0:T(8,128)(2,1)}), bf16[64,8,80]{2,1,0:T(8,128)(2,1)S(1)}, u32[]{:S(2)}, u32[]{:S(2)}) %all-to-all-start) | async-done | bytes 81952 | tf_op jit(solution)/shard_map/all_to_all | solution.py:49
  215.2 0.2 reshape.47
  215.4 0.2 multiply_reduce_fusion
  215.6 0.3 convolution_convert_fusion.1
  216.0 20.6 %all_to_all.23 = bf16[64,2,640]{2,1,0:T(2,128)(2,1)S(1)} all-to-all(bf16[64,2,640]{2,1,0:T(2,128)(2,1)S(1)} %reshape.43), channel_id=1, replica_groups=mesh['head'=8,'expert'=64] {'expert'}, dimensions={0} | all-to-all | bytes 327680 | tf_op jit(solution)/shard_map/all_to_all | solution.py:78
  236.6 0.7 reshape.44
  237.4 24.3 %all-gather.5.cloned.1.call-done = bf16[128,5120]{1,0:T(8,128)(2,1)} async-done(((bf16[128,640]{1,0:T(8,128)(2,1)}), bf16[128,5120]{1,0:T(8,128)(2,1)}) %all-gather.5.cloned.1.call-update) | async-done | bytes 1310736 | tf_op jit(solution)/shard_map/all_gather | solution.py:80
  261.6 2.0 fusion.1
  263.6 1.7 convolution_convert_fusion
  265.4 1.5 copy.22
  266.9 40.3 %reduce-scatter.4.cloned.1.call-done = bf16[640,128]{1,0:T(8,128)(2,1)} async-done(((bf16[5120,128]{1,0:T(8,128)(2,1)}), bf16[640,128]{1,0:T(8,128)(2,1)}) %reduce-scatter.4.cloned.1.call-update) | async-done | bytes 163856
  307.2 1.1 copy.23
  308.2 0.7 reshape.45
  309.0 14.4 %all-to-all-start.2 = ((bf16[64,2,640]{2,1,0:T(2,128)(2,1)}), bf16[64,2,640]{2,1,0:T(2,128)(2,1)S(1)}, u32[]{:S(2)}, u32[]{:S(2)}) async-start(bf16[64,2,640]{2,1,0:T(2,128)(2,1)} %reshape.45), calls=%async_computation.2 | async-start | bytes 327680 | tf_op jit(solution)/shard_map/all_to_all | solution.py:88
  323.4 0.1 copy.21
  323.5 0.1 select_reduce_fusion
  323.6 18.6 %all-to-all-done.2 = bf16[64,2,640]{2,1,0:T(2,128)(2,1)S(1)} async-done(((bf16[64,2,640]{2,1,0:T(2,128)(2,1)}), bf16[64,2,640]{2,1,0:T(2,128)(2,1)S(1)}, u32[]{:S(2)}, u32[]{:S(2)}) %all-to-all-start.2) | async-done | bytes 163872 | tf_op jit(solution)/shard_map/all_to_all | solution.py:88
  342.2 0.8 convolution_add_fusion.1
  (26 shorter events, 0.7 us)
Async XLA Ops:
  6.5 255.1 %copy-start = (bf16[1,2,96,5120]{3,2,1,0:T(8,128)(2,1)S(1)}, bf16[1,2,96,5120]{3,2,1,0:T(8,128)(2,1)}, u32[]{:S(2)}) copy-start(bf16[1,2,96,5120]{3,2,1,0:T(8,128)(2,1)} %param.22) | copy-start | bytes 5898244
  6.5 5.3 %copy-start.3 = (s32[8,6]{1,0:T(8,128)S(1)}, s32[8,6]{1,0:T(8,128)}, u32[]{:S(2)}) copy-start(s32[8,6]{1,0:T(8,128)} %param.20) | copy-start | bytes 580
  6.5 148.3 %copy-start.1 = (bf16[4096,80]{0,1:T(8,128)(2,1)S(1)}, bf16[4096,80]{0,1:T(8,128)(2,1)}, u32[]{:S(2)}) copy-start(bf16[4096,80]{0,1:T(8,128)(2,1)} %param.17) | copy-start | bytes 1966084
  6.5 148.3 %all-gather.3.cloned.1.call-start = ((), (), s32[]{:S(2)}) async-start(), calls=%async_computation.4 | async-start | bytes 4259840 | tf_op jit(solution)/shard_map/all_gather | solution.py:44
  158.4 57.0 %copy-start.2 = (bf16[8,5120]{1,0:T(8,128)(2,1)S(1)}, bf16[8,5120]{1,0:T(8,128)(2,1)}, u32[]{:S(2)}) copy-start(bf16[8,5120]{1,0:T(8,128)(2,1)} %param.18) | copy-start | bytes 245764
  190.4 24.8 %all-to-all-start = ((bf16[64,8,80]{2,1,0:T(8,128)(2,1)}), bf16[64,8,80]{2,1,0:T(8,128)(2,1)S(1)}, u32[]{:S(2)}, u32[]{:S(2)}) async-start(bf16[64,8,80]{2,1,0:T(8,128)(2,1)} %bitcast), calls=%async_computation | async-start | bytes 262144 | tf_op jit(solution)/shard_map/all_to_all | solution.py:49
  199.0 62.6 %all-gather.5.cloned.1.call-start = ((), (), s32[]{:S(2)}) async-start(), calls=%async_computation.5 | async-start | bytes 1474560 | tf_op jit(solution)/shard_map/all_gather | solution.py:80
  237.3 69.9 %reduce-scatter.4.cloned.1.call-start = ((), (), s32[]{:S(2)}) async-start(), calls=%async_computation.6 | async-start | bytes 1474560
  265.4 58.0 %copy-start.4 = (f32[8,6]{1,0:T(8,128)S(1)}, f32[8,6]{1,0:T(8,128)}, u32[]{:S(2)}) copy-start(f32[8,6]{1,0:T(8,128)} %param.21) | copy-start | bytes 580
  309.0 33.2 %all-to-all-start.2 = ((bf16[64,2,640]{2,1,0:T(2,128)(2,1)}), bf16[64,2,640]{2,1,0:T(2,128)(2,1)S(1)}, u32[]{:S(2)}, u32[]{:S(2)}) async-start(bf16[64,2,640]{2,1,0:T(2,128)(2,1)} %reshape.45), calls=%async_computation.2 | async-start | bytes 327680 | tf_op jit(solution)/shard_map/all_to_all | solution.py:88
Sparse Core Ops, SparseCore 0:
  11.9 142.8 all-gather.2
  237.4 24.1 all-gather.4
  267.0 40.1 reduce-scatter.3
where the time goes:
time: 350 us
  waiting for transfers between devices  241 us (69%)
  blocking collectives  51.8 us (15%)
  starting transfers between devices  23.1 us (7%)
  between operations  13.2 us (4%)
  matrix products  12.8 us (4%)
  local copies, waits for them, and re-layouts  6.85 us (2%)
    all_gather x1, waiting for transfers between devices, on_device(): lax.all_gather(flattened, 'expert', axis=0, tiled=True)  143 us
    unnamed x4, waiting for transfers between devices  40.4 us
    psum x1, blocking collectives, on_device(): column_sums = lax.psum(column_terms, 'head')  31.2 us
    all_gather x1, waiting for transfers between devices, on_device(): flat_rows = lax.all_gather(arrived_cols, 'head', axis=1, tiled=True)  24.3 us
    all_to_all x1, blocking collectives, on_device(): lax.all_to_all(outgoing, 'expert', split_axis=0, concat_axis=0, tiled=True)  20.6 us
    all_to_all x1, waiting for transfers between devices, on_device(): lax.all_to_all(summed_rows, 'expert', split_axis=0, concat_axis=0, tiled=...  18.6 us
    all_to_all x1, waiting for transfers between devices, on_device(): lax.all_to_all(column_sums.astype(jnp.bfloat16), 'expert', split_axis=0,...  15.2 us
    all_to_all x1, starting transfers between devices, on_device(): lax.all_to_all(summed_rows, 'expert', split_axis=0, concat_axis=0, tiled=...  14.4 us
  transfers between devices with their start and end apart: 5, of which 5 were waited for; matrix products, arithmetic and copies ran while one was open for 0% of the time, Pallas kernels for 0%

commit v1 on v0

--- a/solution.py
+++ b/solution.py
@@ -5,6 +5,10 @@
 
 softmax_scale = 192.0 ** (-0.5)
 norm_epsilon = 1e-06
+
+
+def _recast_teams(unit):
+    return jnp.sum(jax.lax.all_gather(unit, axis_name="head"), 0)
 
 
 def attend(q_latent, q_rotary, cache_latent, cache_rotary, lengths):
@@ -45,7 +49,7 @@
         w_value_out,
         preferred_element_type=jnp.float32,
     )
-    column_sums = lax.psum(column_terms, "head")
+    column_sums = _recast_teams(column_terms)
     attention = lax.all_to_all(
         column_sums.astype(jnp.bfloat16), "expert", split_axis=0, concat_axis=1, tiled=True
     )

time: 350 us -> 361 us (1.031)
  waiting for transfers between devices: 241 us -> 274 us
  blocking collectives: 51.8 us -> 21.3 us
  starting transfers between devices: 23.1 us -> 29.7 us
    all_gather x0 -> x1, waiting for transfers between devices: none -> 32.9 us  [_recast_teams(): return jnp.sum(jax.lax.all_gather(unit, axis_name='head'), 0)]
    psum x1 -> x0, blocking collectives: 31.2 us -> none  [on_device(): column_sums = lax.psum(column_terms, 'head')]
    all_to_all x1, starting transfers between devices: 8.61 us -> 15.2 us  [on_device(): lax.all_to_all(column_sums.astype(jnp.bfloat16), 'expert', split_axis=0,...]
    unnamed x4 -> x5, waiting for transfers between devices: 40.4 us -> 40.4 us
  transfers between devices with their start and end apart: 5 -> 6, of which waited for: 5 -> 6; matrix products, arithmetic and copies ran while one was open for 0% -> 0% of each run, Pallas kernels for 0% -> 0%
where the time goes in v1:
time: 361 us
  waiting for transfers between devices  274 us (76%)
  starting transfers between devices  29.7 us (8%)
  blocking collectives  21.3 us (6%)
  between operations  13.3 us (4%)
  matrix products  12.4 us (3%)
  local copies, waits for them, and re-layouts  9 us (2%)
    all_gather x1, waiting for transfers between devices, on_device(): lax.all_gather(flattened, 'expert', axis=0, tiled=True)  143 us
    unnamed x5, waiting for transfers between devices  40.4 us
    all_gather x1, waiting for transfers between devices, _recast_teams(): return jnp.sum(jax.lax.all_gather(unit, axis_name='head'), 0)  32.9 us
    all_gather x1, waiting for transfers between devices, on_device(): flat_rows = lax.all_gather(arrived_cols, 'head', axis=1, tiled=True)  24.7 us
    all_to_all x1, blocking collectives, on_device(): lax.all_to_all(outgoing, 'expert', split_axis=0, concat_axis=0, tiled=True)  21.3 us
    all_to_all x1, waiting for transfers between devices, on_device(): lax.all_to_all(summed_rows, 'expert', split_axis=0, concat_axis=0, tiled=...  18.5 us
    all_to_all x1, starting transfers between devices, on_device(): lax.all_to_all(column_sums.astype(jnp.bfloat16), 'expert', split_axis=0,...  15.2 us
    all_to_all x1, waiting for transfers between devices, on_device(): lax.all_to_all(column_sums.astype(jnp.bfloat16), 'expert', split_axis=0,...  14.5 us
  transfers between devices with their start and end apart: 6, of which 6 were waited for; matrix products, arithmetic and copies ran while one was open for 0% of the time, Pallas kernels for 0%

profile of v1, /device:TPU:7, one launch (start us, length us, event | category | flops | bytes accessed | tf_op | source)
XLA Modules:
  0.0 360.8 jit_solution(6892368965744753505)
XLA Ops:
  6.5 1.8 fusion.21
  8.3 1.1 fusion.8
  9.4 0.2 fusion.20
  9.6 0.3 fusion.4
  9.9 0.7 copy.22
  10.6 143.0 %all-gather.5.cloned.1.call-done = bf16[512,4096]{1,0:T(8,128)(2,1)} async-done(((bf16[8,4096]{1,0:T(8,128)(2,1)}), bf16[512,4096]{1,0:T(8,128)(2,1)}) %all-gather.5.cloned.1.call-update) | async-done | bytes 4194320 | tf_op jit(solution)/shard_map/all_gather | solution.py:48
  153.6 4.4 %fusion.22 = f32[512,80]{0,1:T(8,128)} fusion(bf16[512,4096]{1,0:T(8,128)(2,1)} %all-gather.5.cloned.1.call-done, bf16[4096,80]{0,1:T(8,128)(2,1)} %param.17), kind=kOutput, calls=%fused_computation.41 | convolution fusion | flops 335544320 | bytes 5013504 | tf_op jit(solution)/shard_map/dot_general | solution.py:47
  158.3 0.2 select_reduce_fusion.1
  158.6 32.9 %all-gather.9.cloned.1.call-done = f32[4096,80]{0,1:T(8,128)} async-done(((f32[512,80]{0,1:T(8,128)}), f32[4096,80]{0,1:T(8,128)}) %all-gather.9.cloned.1.call-update) | async-done | bytes 1310736 | tf_op jit(solution)/shard_map/all_gather | solution.py:11
  191.5 2.1 copy.23
  193.6 0.3 bitcast_reduce_fusion
  194.0 0.7 copy.16
  194.7 15.2 %all-to-all-start = ((bf16[64,8,80]{2,1,0:T(8,128)(2,1)}), bf16[64,8,80]{2,1,0:T(8,128)(2,1)S(1)}, u32[]{:S(2)}, u32[]{:S(2)}) async-start(bf16[64,8,80]{2,1,0:T(8,128)(2,1)} %bitcast), calls=%async_computation | async-start | bytes 262144 | tf_op jit(solution)/shard_map/all_to_all | solution.py:53
  209.9 0.1 copy.18
  210.0 0.8 dynamic-slice
  210.8 14.5 %all-to-all-done = bf16[64,8,80]{2,1,0:T(8,128)(2,1)S(1)} async-done(((bf16[64,8,80]{2,1,0:T(8,128)(2,1)}), bf16[64,8,80]{2,1,0:T(8,128)(2,1)S(1)}, u32[]{:S(2)}, u32[]{:S(2)}) %all-to-all-start) | async-done | bytes 81952 | tf_op jit(solution)/shard_map/all_to_all | solution.py:53
  225.4 0.2 reshape.49
  225.6 0.2 multiply_reduce_fusion
  225.7 0.3 convolution_convert_fusion.1
  226.1 21.3 %all_to_all.20 = bf16[64,2,640]{2,1,0:T(2,128)(2,1)S(1)} all-to-all(bf16[64,2,640]{2,1,0:T(2,128)(2,1)S(1)} %reshape.45), channel_id=1, replica_groups=mesh['head'=8,'expert'=64] {'expert'}, dimensions={0} | all-to-all | bytes 327680 | tf_op jit(solution)/shard_map/all_to_all | solution.py:82
  247.5 0.7 reshape.46
  248.3 24.7 %all-gather.7.cloned.1.call-done = bf16[128,5120]{1,0:T(8,128)(2,1)} async-done(((bf16[128,640]{1,0:T(8,128)(2,1)}), bf16[128,5120]{1,0:T(8,128)(2,1)}) %all-gather.7.cloned.1.call-update) | async-done | bytes 1310736 | tf_op jit(solution)/shard_map/all_gather | solution.py:84
  273.0 2.0 fusion.1
  275.0 1.7 convolution_convert_fusion
  276.7 1.5 copy.20
  278.2 40.3 %reduce-scatter.4.cloned.1.call-done = bf16[640,128]{1,0:T(8,128)(2,1)} async-done(((bf16[5120,128]{1,0:T(8,128)(2,1)}), bf16[640,128]{1,0:T(8,128)(2,1)}) %reduce-scatter.4.cloned.1.call-update) | async-done | bytes 163856
  318.5 1.1 copy.21
  319.6 0.7 reshape.47
  320.3 14.4 %all-to-all-start.2 = ((bf16[64,2,640]{2,1,0:T(2,128)(2,1)}), bf16[64,2,640]{2,1,0:T(2,128)(2,1)S(1)}, u32[]{:S(2)}, u32[]{:S(2)}) async-start(bf16[64,2,640]{2,1,0:T(2,128)(2,1)} %reshape.47), calls=%async_computation.2 | async-start | bytes 327680 | tf_op jit(solution)/shard_map/all_to_all | solution.py:92
  334.8 0.1 copy.19
  334.9 18.5 %all-to-all-done.2 = bf16[64,2,640]{2,1,0:T(2,128)(2,1)S(1)} async-done(((bf16[64,2,640]{2,1,0:T(2,128)(2,1)}), bf16[64,2,640]{2,1,0:T(2,128)(2,1)S(1)}, u32[]{:S(2)}, u32[]{:S(2)}) %all-to-all-start.2) | async-done | bytes 163872 | tf_op jit(solution)/shard_map/all_to_all | solution.py:92
  353.5 0.8 convolution_add_fusion.1
  (30 shorter events, 0.9 us)
Async XLA Ops:
  6.5 266.5 %copy-start = (bf16[1,2,96,5120]{3,2,1,0:T(8,128)(2,1)S(1)}, bf16[1,2,96,5120]{3,2,1,0:T(8,128)(2,1)}, u32[]{:S(2)}) copy-start(bf16[1,2,96,5120]{3,2,1,0:T(8,128)(2,1)} %param.22) | copy-start | bytes 5898244
  6.5 3.0 copy-start.1
  6.5 147.1 %all-gather.5.cloned.1.call-start = ((), (), s32[]{:S(2)}) async-start(), calls=%async_computation.4 | async-start | bytes 4259840 | tf_op jit(solution)/shard_map/all_gather | solution.py:48
  10.6 147.5 %copy-start.3 = (s32[8,6]{1,0:T(8,128)S(1)}, s32[8,6]{1,0:T(8,128)}, u32[]{:S(2)}) copy-start(s32[8,6]{1,0:T(8,128)} %param.20) | copy-start | bytes 580
  10.6 180.9 %all-gather.9.cloned.1.call-start = ((), (), s32[]{:S(2)}) async-start(), calls=%async_computation.6 | async-start | bytes 1474560 | tf_op jit(solution)/shard_map/all_gather | solution.py:11
  193.6 32.0 %copy-start.2 = (bf16[8,5120]{1,0:T(8,128)(2,1)S(1)}, bf16[8,5120]{1,0:T(8,128)(2,1)}, u32[]{:S(2)}) copy-start(bf16[8,5120]{1,0:T(8,128)(2,1)} %param.18) | copy-start | bytes 245764
  194.7 30.6 %all-to-all-start = ((bf16[64,8,80]{2,1,0:T(8,128)(2,1)}), bf16[64,8,80]{2,1,0:T(8,128)(2,1)S(1)}, u32[]{:S(2)}, u32[]{:S(2)}) async-start(bf16[64,8,80]{2,1,0:T(8,128)(2,1)} %bitcast), calls=%async_computation | async-start | bytes 262144 | tf_op jit(solution)/shard_map/all_to_all | solution.py:53
  209.9 63.1 %all-gather.7.cloned.1.call-start = ((), (), s32[]{:S(2)}) async-start(), calls=%async_computation.5 | async-start | bytes 1474560 | tf_op jit(solution)/shard_map/all_gather | solution.py:84
  248.2 70.3 %reduce-scatter.4.cloned.1.call-start = ((), (), s32[]{:S(2)}) async-start(), calls=%async_computation.7 | async-start | bytes 1474560
  278.2 56.6 %copy-start.4 = (f32[8,6]{1,0:T(8,128)S(1)}, f32[8,6]{1,0:T(8,128)}, u32[]{:S(2)}) copy-start(f32[8,6]{1,0:T(8,128)} %param.21) | copy-start | bytes 580
  320.3 33.1 %all-to-all-start.2 = ((bf16[64,2,640]{2,1,0:T(2,128)(2,1)}), bf16[64,2,640]{2,1,0:T(2,128)(2,1)S(1)}, u32[]{:S(2)}, u32[]{:S(2)}) async-start(bf16[64,2,640]{2,1,0:T(2,128)(2,1)} %reshape.47), calls=%async_computation.2 | async-start | bytes 327680 | tf_op jit(solution)/shard_map/all_to_all | solution.py:92
Sparse Core Ops, SparseCore 0:
  10.7 142.8 all-gather.4
  158.2 33.2 all-gather.8
  248.3 24.6 all-gather.6
  278.3 40.1 reduce-scatter.3
